TPU v7x, 32 devices: a whole 2x2x4 slice. The times are simulated.
32 devices in a mesh: pipe: 4 (over z), et: 8 (over y, x, core).
Axes of the slice: x: 2, y: 2, z: 4, core: 2. Of those that a mesh axis runs over, the one named last changes fastest.
Arguments:
- tokens: bfloat16 [4, 1024, 4096], P('pipe', 'et'), may hold values from -6 to 6
- gate_vals: bfloat16 [4, 1024, 2], P('pipe', 'et'), may hold values from 0.099609375 to 1
- expert_ids: int32 [4, 1024, 2], P('pipe', 'et'), may hold values from 0 to 7, as said below
- grad_out: bfloat16 [4, 1024, 4096], P('pipe', 'et'), may hold values from -6 to 6
- w_gate: bfloat16 [4, 2, 4096, 7168], P('pipe', None, None, 'et'), may hold values from -0.09375 to 0.09375
- w_up: bfloat16 [4, 2, 4096, 7168], P('pipe', None, None, 'et'), may hold values from -0.09375 to 0.09375
- w_down: bfloat16 [4, 2, 7168, 4096], P('pipe', None, 'et'), may hold values from -0.0625 to 0.0625
Outputs:
- moe_out: bfloat16 [4, 1024, 4096], P('pipe', 'et')
- prior_grads: bfloat16 [4, 1024, 4096], P('pipe', 'et')
Inputs may be any that keep to these rules, and one draw needn't show every extreme that they name: `expert_ids`: each row names 2 different experts. The rows of one device of one section name each of experts 0 to 1 at most 16 times, and for each of these experts there is a section in which every device's rows name it exactly 16 times.
All inputs are finite; a program needn't handle non-finite values.
Results may differ from a plain program's by a relative error of at most 0.012.
Values may be sent and summed in bfloat16 or wider, within the bound.
No kernel may reach another device: no remote copies, remote signals or barrier semaphores. Data moves between devices by JAX's collectives and lax.ppermute only.
A program may use at most 192 MiB of HBM per device.

v0:
```python
import jax
import jax.numpy as jnp
from jax import lax
from jax.sharding import PartitionSpec as P

E_WIN = 2
MOST = 16
TAIL = 128


def shifted(value, axis, steps):
    count = lax.axis_size(axis)
    first, last = (max(0, -steps), min(count, count - steps))
    return lax.ppermute(value, axis, [(source, source + steps) for source in range(first, last)])


def silu_parts(pre_gate):
    sigma = jax.nn.sigmoid(pre_gate)
    return (pre_gate * sigma, sigma * (1.0 + pre_gate * (1.0 - sigma)))


def local_slots(local_routes, local_gates):
    slot_ids = jnp.arange(MOST, dtype=jnp.int32)[:, None]
    selects, weights = ([], [])
    for expert in range(E_WIN):
        matches = local_routes == expert
        routed = jnp.any(matches, axis=1)
        gate_val = jnp.sum(jnp.where(matches, local_gates.astype(jnp.float32), 0.0), axis=1)
        positions = jnp.cumsum(routed.astype(jnp.int32), dtype=jnp.int32) - 1
        select = routed[None, :] & (positions[None, :] == slot_ids)
        selects.append(select)
        weights.append(jnp.sum(jnp.where(select, gate_val[None, :], 0.0), axis=1))
    return (jnp.concatenate(selects, axis=0), jnp.concatenate(weights))


def pick_rows(select, rows):
    return jnp.dot(select.astype(rows.dtype), rows, preferred_element_type=jnp.float32).astype(
        rows.dtype
    )


def halve_over_et(parts):
    n = lax.axis_size("et")
    me = lax.axis_index("et")
    held = parts
    bit = 1
    while 2 * bit < n:
        halves = held.reshape((held.shape[0] // 2, 2) + held.shape[1:])
        side = me // bit % 2
        keep = jnp.take(halves, side, axis=1)
        give = jnp.take(halves, 1 - side, axis=1)
        got = lax.ppermute(give, "et", [(i, i ^ bit) for i in range(n)])
        held = (keep.astype(jnp.float32) + got.astype(jnp.float32)).astype(jnp.bfloat16)
        bit *= 2
    side = me // bit % 2
    return (jnp.take(held, side, axis=0), jnp.take(held, 1 - side, axis=0), bit)


def reduce_to_owner(parts):
    n = lax.axis_size("et")
    keep, give, bit = halve_over_et(parts)
    got = lax.ppermute(give, "et", [(i, i ^ bit) for i in range(n)])
    return keep.astype(jnp.float32) + got.astype(jnp.float32)


def reduce_to_previous(parts):
    n = lax.axis_size("et")
    stages = lax.axis_size("pipe")
    keep, give, bit = halve_over_et(parts)
    to_same = [(stage * n + i, (stage - 1) * n + i) for stage in range(1, stages) for i in range(n)]
    to_other = [
        (stage * n + i, (stage - 1) * n + (i ^ bit)) for stage in range(1, stages) for i in range(n)
    ]
    first = lax.ppermute(keep, ("pipe", "et"), to_same)
    second = lax.ppermute(give, ("pipe", "et"), to_other)
    return first.astype(jnp.float32) + second.astype(jnp.float32)


def unpack(slot_sums, select):
    return lax.dot_general(
        select.astype(jnp.float32),
        slot_sums,
        (((0,), (0,)), ((), ())),
        precision=lax.Precision.HIGHEST,
        preferred_element_type=jnp.float32,
    ).astype(jnp.bfloat16)


def per_device(tokens, gate_vals, expert_ids, grad_out, w_gate, w_up, w_down):
    local_rows = tokens[0]
    local_grads = grad_out[0]
    gate_mats = w_gate[0]
    up_mats = w_up[0]
    down_mats = w_down[0]
    n = lax.axis_size("et")
    width = local_rows.shape[1]
    select, weights = local_slots(expert_ids[0], gate_vals[0])
    next_routes = shifted(expert_ids[0], "pipe", -1)
    next_select = local_slots(next_routes, gate_vals[0])[0]
    weight_cols = jnp.broadcast_to(weights.astype(jnp.bfloat16)[:, None], (E_WIN * MOST, TAIL))
    packed = jnp.concatenate(
        [pick_rows(select, local_rows), pick_rows(select, local_grads), weight_cols], axis=1
    )
    gathered = lax.all_gather(packed, "et", axis=0, tiled=True).reshape(
        n, E_WIN, MOST, 2 * width + TAIL
    )
    outs = []
    stored = []
    for expert in range(E_WIN):
        rows = gathered[:, expert, :, :width].reshape(n * MOST, width)
        gate_w = gathered[:, expert, :, 2 * width].reshape(n * MOST, 1).astype(jnp.float32)
        pre_gate = jnp.dot(rows, gate_mats[expert], preferred_element_type=jnp.float32)
        pre_up = jnp.dot(rows, up_mats[expert], preferred_element_type=jnp.float32)
        activated, slopes = silu_parts(pre_gate)
        hidden = (activated * pre_up).astype(jnp.bfloat16)
        out_e = gate_w * jnp.dot(hidden, down_mats[expert], preferred_element_type=jnp.float32)
        outs.append(out_e.astype(jnp.bfloat16).reshape(n, MOST, width))
        stored.append((gate_w, pre_up, activated, slopes))
    out_parts = jnp.stack(outs, axis=1).reshape(n, E_WIN * MOST, width)
    out_sums = reduce_to_owner(out_parts)
    grad_outs = []
    for expert in range(E_WIN):
        gate_w, pre_up, activated, slopes = stored[expert]
        grad_rows = gathered[:, expert, :, width : 2 * width].reshape(n * MOST, width)
        d_hidden = gate_w * lax.dot_general(
            grad_rows,
            down_mats[expert],
            (((1,), (1,)), ((), ())),
            preferred_element_type=jnp.float32,
        )
        d_gate = (d_hidden * pre_up * slopes).astype(jnp.bfloat16)
        d_up = (d_hidden * activated).astype(jnp.bfloat16)
        grad_e = lax.dot_general(
            d_gate, gate_mats[expert], (((1,), (1,)), ((), ())), preferred_element_type=jnp.float32
        ) + lax.dot_general(
            d_up, up_mats[expert], (((1,), (1,)), ((), ())), preferred_element_type=jnp.float32
        )
        grad_outs.append(grad_e.astype(jnp.bfloat16).reshape(n, MOST, width))
    grad_parts = jnp.stack(grad_outs, axis=1).reshape(n, E_WIN * MOST, width)
    out_sums, grad_parts = lax.optimization_barrier((out_sums, grad_parts))
    received = unpack(reduce_to_previous(grad_parts), next_select)
    out_share = unpack(out_sums, select)
    return (out_share[None], received[None])


def solution(mesh):
    placed = (
        P("pipe", "et", None),
        P("pipe", "et", None),
        P("pipe", "et", None),
        P("pipe", "et", None),
        P("pipe", None, None, "et"),
        P("pipe", None, None, "et"),
        P("pipe", None, "et", None),
    )
    return jax.shard_map(
        per_device,
        mesh=mesh,
        in_specs=placed,
        out_specs=(P("pipe", "et", None), P("pipe", "et", None)),
        check_vma=False,
    )
```

profile of v0, /device:TPU:0, one launch (start us, length us, event | category | flops | bytes accessed | tf_op | source)
XLA Modules:
  0.0 167.1 jit_solution(3968941739426077450)
XLA Ops:
  9.8 1.5 convolution_convert_fusion.3
  12.6 39.7 %all-gather.2.cloned.1.call-done = bf16[256,8320]{1,0:T(8,128)(2,1)} async-done(((bf16[32,8320]{1,0:T(8,128)(2,1)}), bf16[256,8320]{1,0:T(8,128)(2,1)}) %all-gather.2.cloned.1.call-update) | async-done | bytes 4259856 | tf_op jit(solution)/shard_map/all_gather | solution.py:104
  53.3 2.9 %fusion.103 = (bf16[8,1,16,4096]{3,2,1,0:T(8,128)(2,1)S(1)}, bf16[8,1,16,4096]{3,2,1,0:T(8,128)(2,1)S(1)}, bf16[8,1,16,4096]{3,2,1,0:T(8,128)(2,1)S(1)}, bf16[8,1,16,4096]{3,2,1,0:T(8,128)(2,1)S(1)}) fusion(bf16[8,2,16,8320]{3,2,1,0:T(8,128)(2,1)} %bitcast.175), kind=kLoop, calls=%fused_computation.132 | loop fusion | bytes 8388608 | tf_op jit(solution)/shard_map/slice | solution.py:124
  56.2 5.2 %fusion.6 = f32[128,896]{1,0:T(8,128)S(1)} fusion(bf16[128,4096]{1,0:T(8,128)(2,1)S(1)} %bitcast.188, bf16[1,2,4096,896]{3,2,1,0:T(8,128)(2,1)} %param.18), kind=kOutput, calls=%fused_computation.6 | convolution fusion | flops 939524096 | bytes 8847360 | tf_op jit(solution)/shard_map/dot_general | solution.py:113
  61.4 2.1 %fusion.10 = f32[128,896]{1,0:T(8,128)} fusion(bf16[128,4096]{1,0:T(8,128)(2,1)S(1)} %bitcast.189, bf16[1,2,4096,896]{3,2,1,0:T(8,128)(2,1)S(1)} %copy-done.3), kind=kOutput, calls=%fused_computation.10 | convolution fusion | flops 939524096 | bytes 8847360 | tf_op jit(solution)/shard_map/dot_general | solution.py:112
  68.5 4.7 %fusion.48 = bf16[128,4096]{1,0:T(8,128)(2,1)S(1)} fusion(bf16[1,2,896,4096]{3,2,1,0:T(8,128)(2,1)} %param.19, f32[128]{0:T(128)S(1)} %reshape.401, f32[128,896]{1,0:T(8,128)S(1)} %fusion.6, f32[128,896]{1,0:T(8,128)} %fusion.10), kind=kOutput, calls=%fused_computation.40 | convolution fusion | flops 941260800 | bytes 9306624 | tf_op jit(solution)/shard_map/dot_general | solution.py:116
  73.2 4.5 %fusion.54 = bf16[128,4096]{1,0:T(8,128)(2,1)S(1)} fusion(bf16[1,2,896,4096]{3,2,1,0:T(8,128)(2,1)} %param.19, f32[128]{0:T(128)S(1)} %reshape.400, f32[128,896]{1,0:T(8,128)S(1)} %fusion.18, f32[128,896]{1,0:T(8,128)S(1)} %fusion.22), kind=kOutput, calls=%fused_computation.42 | convolution fusion | flops 941260800 | bytes 9306624 | tf_op jit(solution)/shard_map/dot_general | solution.py:116
  78.4 2.4 %fusion.65 = f32[128,896]{1,0:T(8,128)S(1)} fusion(bf16[128,4096]{1,0:T(8,128)(2,1)S(1)} %bitcast.185, bf16[1,2,896,4096]{3,2,1,0:T(8,128)(2,1)S(1)} %bitcast.192, f32[128]{0:T(128)S(1)} %reshape.401), kind=kOutput, calls=%fused_computation.55 | convolution fusion | flops 939638784 | bytes 8847872 | tf_op jit(solution)/shard_map/dot_general | solution.py:125
  80.9 5.7 %fusion.4 = f32[128,4096]{1,0:T(8,128)S(1)} fusion(bf16[1,2,4096,896]{3,2,1,0:T(8,128)(2,1)} %param.18, f32[128,896]{1,0:T(8,128)S(1)} %fusion.65, f32[128,896]{1,0:T(8,128)S(1)} %copy-done.4), kind=kOutput, calls=%fused_computation.4 | convolution fusion | flops 940212224 | bytes 10354688 | tf_op jit(solution)/shard_map/dot_general | solution.py:135
  86.6 2.4 %fusion.62 = f32[128,896]{1,0:T(8,128)S(1)} fusion(bf16[128,4096]{1,0:T(8,128)(2,1)S(1)} %bitcast.184, bf16[1,2,896,4096]{3,2,1,0:T(8,128)(2,1)S(1)} %bitcast.192, f32[128]{0:T(128)S(1)} %reshape.400), kind=kOutput, calls=%fused_computation.54 | convolution fusion | flops 939638784 | bytes 8847872 | tf_op jit(solution)/shard_map/dot_general | solution.py:125
  89.0 5.5 %fusion.16 = f32[128,4096]{1,0:T(8,128)S(1)} fusion(bf16[1,2,4096,896]{3,2,1,0:T(8,128)(2,1)} %param.18, f32[128,896]{1,0:T(8,128)S(1)} %fusion.62, f32[128,896]{1,0:T(8,128)S(1)} %fusion.22), kind=kOutput, calls=%fused_computation.16 | convolution fusion | flops 940212224 | bytes 10354688 | tf_op jit(solution)/shard_map/dot_general | solution.py:135
  94.5 5.6 %fusion.51 = bf16[128,4096]{1,0:T(8,128)(2,1)S(1)} fusion(f32[128,4096]{1,0:T(8,128)S(1)} %fusion.4, bf16[1,2,4096,896]{3,2,1,0:T(8,128)(2,1)} %param.17, f32[128,896]{1,0:T(8,128)S(1)} %copy-done.4, f32[128,896]{1,0:T(8,128)S(1)} %fusion.65, f32[128,896]{1,0:T(8,128)S(1)} %fusion.6), kind=kOutput, calls=%fused_computation.41 | convolution fusion | flops 941719552 | bytes 11862016 | tf_op jit(solution)/shard_map/dot_general | solution.py:133
  100.5 1.5 collective-permute-start.1
  102.1 5.6 %fusion.57 = bf16[128,4096]{1,0:T(8,128)(2,1)S(1)} fusion(f32[128,4096]{1,0:T(8,128)S(1)} %fusion.16, bf16[1,2,4096,896]{3,2,1,0:T(8,128)(2,1)} %param.17, f32[128,896]{1,0:T(8,128)S(1)} %fusion.22, f32[128,896]{1,0:T(8,128)S(1)} %fusion.62, f32[128,896]{1,0:T(8,128)S(1)} %fusion.18), kind=kOutput, calls=%fused_computation.43 | convolution fusion | flops 941719552 | bytes 11862016 | tf_op jit(solution)/shard_map/dot_general | solution.py:133
  107.7 7.0 %collective-permute-done.1 = bf16[2,32,4096]{2,1,0:T(8,128)(2,1)S(1)} collective-permute-done((bf16[2,32,4096]{2,1,0:T(8,128)(2,1)S(1)}, bf16[2,32,4096]{2,1,0:T(8,128)(2,1)S(1)}, u32[]{:S(2)}, u32[]{:S(2)}) %collective-permute-start.1) | collective-permute-done | bytes 524320 | tf_op jit(solution)/shard_map/ppermute | solution.py:52
  114.9 1.4 collective-permute-start.2
  116.5 6.1 %collective-permute-done.2 = bf16[32,4096]{1,0:T(8,128)(2,1)S(1)} collective-permute-done((bf16[32,4096]{1,0:T(8,128)(2,1)S(1)}, bf16[32,4096]{1,0:T(8,128)(2,1)S(1)}, u32[]{:S(2)}, u32[]{:S(2)}) %collective-permute-start.2) | collective-permute-done | bytes 262176 | tf_op jit(solution)/shard_map/ppermute | solution.py:62
  124.2 4.2 %collective-permute-done.3 = s32[128,2]{0,1:T(2,128)S(1)} collective-permute-done((s32[128,2]{0,1:T(2,128)S(1)}, s32[128,2]{0,1:T(2,128)S(1)}, u32[]{:S(2)}, u32[]{:S(2)}) %collective-permute-start.3) | collective-permute-done | bytes 1056 | tf_op jit(solution)/shard_map/ppermute | solution.py:14
  128.8 1.5 collective-permute-start.5
  131.1 11.0 %collective-permute-done.5 = bf16[2,32,4096]{2,1,0:T(8,128)(2,1)} collective-permute-done((bf16[2,32,4096]{2,1,0:T(8,128)(2,1)S(1)}, bf16[2,32,4096]{2,1,0:T(8,128)(2,1)}, u32[]{:S(2)}, u32[]{:S(2)}) %collective-permute-start.5) | collective-permute-done | bytes 524320 | tf_op jit(solution)/shard_map/ppermute | solution.py:52
  146.0 2.0 %fusion.60 = bf16[1,128,4096]{2,1,0:T(8,128)(2,1)} fusion(f32[32,4096]{1,0:T(8,128)S(1)} %convert_add_fusion, pred[16,128]{1,0:T(8,128)(4,1)S(1)} %get-tuple-element.59, pred[16,128]{1,0:T(8,128)(4,1)S(1)} %get-tuple-element.58), kind=kOutput, calls=%fused_computation.46 | convolution fusion | flops 201854976 | bytes 1576960 | tf_op jit(solution)/shard_map/dot_general | solution.py:80
  148.0 7.4 %collective-permute-done.7 = bf16[32,4096]{1,0:T(8,128)(2,1)S(1)} collective-permute-done((bf16[32,4096]{1,0:T(8,128)(2,1)S(1)}, bf16[32,4096]{1,0:T(8,128)(2,1)S(1)}, u32[]{:S(2)}, u32[]{:S(2)}) %collective-permute-start.7) | collective-permute-done | bytes 262176 | tf_op jit(solution)/shard_map/ppermute | solution.py:75
  155.4 2.9 %collective-permute-done.6 = bf16[32,4096]{1,0:T(8,128)(2,1)S(1)} collective-permute-done((bf16[32,4096]{1,0:T(8,128)(2,1)S(1)}, bf16[32,4096]{1,0:T(8,128)(2,1)S(1)}, u32[]{:S(2)}, u32[]{:S(2)}) %collective-permute-start.6) | collective-permute-done | bytes 262176 | tf_op jit(solution)/shard_map/ppermute | solution.py:74
  158.3 2.0 %fusion.61 = bf16[1,128,4096]{2,1,0:T(8,128)(2,1)} fusion(bf16[32,4096]{1,0:T(8,128)(2,1)S(1)} %collective-permute-done.7, bf16[32,4096]{1,0:T(8,128)(2,1)S(1)} %collective-permute-done.6, pred[16,128]{1,0:T(8,128)(4,1)S(1)} %get-tuple-element.61, pred[16,128]{1,0:T(8,128)(4,1)S(1)} %get-tuple-element.60), kind=kOutput, calls=%fused_computation.47 | convolution fusion | flops 202248192 | bytes 1576960 | tf_op jit(solution)/shard_map/dot_general | solution.py:80
  (83 shorter events, 17.7 us)
Async XLA Ops:
  7.2 2.4 %copy-start = (bf16[1,128,4096]{2,1,0:T(8,128)(2,1)S(1)}, bf16[1,128,4096]{2,1,0:T(8,128)(2,1)}, u32[]{:S(2)}) copy-start(bf16[1,128,4096]{2,1,0:T(8,128)(2,1)} %param.16) | copy-start | bytes 3145732
  7.2 45.1 %all-gather.2.cloned.1.call-start = ((), (), s32[]{:S(2)}) async-start(), calls=%async_computation | async-start | bytes 4792320 | tf_op jit(solution)/shard_map/all_gather | solution.py:104
  52.3 9.1 %copy-start.3 = (bf16[1,2,4096,896]{3,2,1,0:T(8,128)(2,1)S(1)}, bf16[1,2,4096,896]{3,2,1,0:T(8,128)(2,1)}, u32[]{:S(2)}) copy-start(bf16[1,2,4096,896]{3,2,1,0:T(8,128)(2,1)} %param.17) | copy-start | bytes 44040196
  53.2 10.3 %slice-start.4 = ((s8[14680064]{0:T(1024)(128)(4,1)}), s8[4194304]{0:T(1024)(128)(4,1)S(1)}, s32[]{:S(2)}) async-start(s8[14680064]{0:T(1024)(128)(4,1)} %bitcast.193), calls=%async_computation.5 | async-start | bytes 8388608
  53.2 10.3 %slice-start.5 = ((s8[14680064]{0:T(1024)(128)(4,1)}), s8[4194304]{0:T(1024)(128)(4,1)S(1)}, s32[]{:S(2)}) async-start(s8[14680064]{0:T(1024)(128)(4,1)} %bitcast.193), calls=%async_computation.6 | async-start | bytes 8388608
  56.2 8.7 %slice-start.6 = ((s8[14680064]{0:T(1024)(128)(4,1)}), s8[4194304]{0:T(1024)(128)(4,1)S(1)}, s32[]{:S(2)}) async-start(s8[14680064]{0:T(1024)(128)(4,1)} %bitcast.193), calls=%async_computation.7 | async-start | bytes 8388608
  61.4 4.0 %slice-start.7 = ((s8[14680064]{0:T(1024)(128)(4,1)}), s8[2097152]{0:T(1024)(128)(4,1)S(1)}, s32[]{:S(2)}) async-start(s8[14680064]{0:T(1024)(128)(4,1)} %bitcast.193), calls=%async_computation.8 | async-start | bytes 4194304
  68.5 9.9 %slice-start = ((s8[14680064]{0:T(1024)(128)(4,1)}), s8[4194304]{0:T(1024)(128)(4,1)S(1)}, s32[]{:S(2)}) async-start(s8[14680064]{0:T(1024)(128)(4,1)} %bitcast.191), calls=%async_computation.1 | async-start | bytes 8388608
  68.5 9.9 %slice-start.1 = ((s8[14680064]{0:T(1024)(128)(4,1)}), s8[4194304]{0:T(1024)(128)(4,1)S(1)}, s32[]{:S(2)}) async-start(s8[14680064]{0:T(1024)(128)(4,1)} %bitcast.191), calls=%async_computation.2 | async-start | bytes 8388608
  73.2 5.2 %slice-start.2 = ((s8[14680064]{0:T(1024)(128)(4,1)}), s8[4194304]{0:T(1024)(128)(4,1)S(1)}, s32[]{:S(2)}) async-start(s8[14680064]{0:T(1024)(128)(4,1)} %bitcast.191), calls=%async_computation.3 | async-start | bytes 8388608
  73.2 5.2 %slice-start.3 = ((s8[14680064]{0:T(1024)(128)(4,1)}), s8[2097152]{0:T(1024)(128)(4,1)S(1)}, s32[]{:S(2)}) async-start(s8[14680064]{0:T(1024)(128)(4,1)} %bitcast.191), calls=%async_computation.4 | async-start | bytes 4194304
  77.9 2.9 %copy-start.4 = (f32[128,896]{1,0:T(8,128)S(1)}, f32[128,896]{1,0:T(8,128)}, u32[]{:S(2)}) copy-start(f32[128,896]{1,0:T(8,128)} %fusion.10) | copy-start | bytes 1376260
  78.1 22.0 %collective-permute-start = (bf16[4,32,4096]{2,1,0:T(8,128)(2,1)S(1)}, bf16[4,32,4096]{2,1,0:T(8,128)(2,1)S(1)}, u32[]{:S(2)}, u32[]{:S(2)}) collective-permute-start(bf16[4,32,4096]{2,1,0:T(8,128)(2,1)S(1)} %select_bitcast_fusion.1), channel_id=1, source_target_pairs={{0,1},{1,0},{2,3},{3,2},{4,5},{5,4},{6,7},{7,6},{8,9},{9,8},{10,11... | collective-permute-start | bytes 3145736 | tf_op jit(solution)/shard_map/ppermute | solution.py:52
  100.5 14.1 %collective-permute-start.1 = (bf16[2,32,4096]{2,1,0:T(8,128)(2,1)S(1)}, bf16[2,32,4096]{2,1,0:T(8,128)(2,1)S(1)}, u32[]{:S(2)}, u32[]{:S(2)}) collective-permute-start(bf16[2,32,4096]{2,1,0:T(8,128)(2,1)S(1)} %select_bitcast_fusion.3), channel_id=1, source_target_pairs={{0,2},{1,3},{2,0},{3,1},{4,6},{5,7},{6,4},{7,5},{8,10},{9,11},{10,... | collective-permute-start | bytes 1572872 | tf_op jit(solution)/shard_map/ppermute | solution.py:52
  107.7 15.2 %copy-start.2 = (s32[1,128,2]{1,2,0:T(2,128)S(1)}, s32[1,128,2]{1,2,0:T(2,128)}, u32[]{:S(2)}) copy-start(s32[1,128,2]{1,2,0:T(2,128)} %param.15) | copy-start | bytes 3076
  114.9 7.7 %collective-permute-start.2 = (bf16[32,4096]{1,0:T(8,128)(2,1)S(1)}, bf16[32,4096]{1,0:T(8,128)(2,1)S(1)}, u32[]{:S(2)}, u32[]{:S(2)}) collective-permute-start(bf16[32,4096]{1,0:T(8,128)(2,1)S(1)} %select_bitcast_fusion.6), channel_id=1, source_target_pairs={{0,4},{1,5},{2,6},{3,7},{4,0},{5,1},{6,2},{7,3},{8,12},{9,13},{10,... | collective-permute-start | bytes 786440 | tf_op jit(solution)/shard_map/ppermute | solution.py:62
  116.3 44.0 %copy-start.1 = (bf16[1,128,4096]{2,1,0:T(8,128)(2,1)S(1)}, bf16[1,128,4096]{2,1,0:T(8,128)(2,1)}, u32[]{:S(2)}) copy-start(bf16[1,128,4096]{2,1,0:T(8,128)(2,1)} %param.16) | copy-start | bytes 3145732
  122.8 5.6 %collective-permute-start.4 = (bf16[4,32,4096]{2,1,0:T(8,128)(2,1)S(1)}, bf16[4,32,4096]{2,1,0:T(8,128)(2,1)S(1)}, u32[]{:S(2)}, u32[]{:S(2)}) collective-permute-start(bf16[4,32,4096]{2,1,0:T(8,128)(2,1)S(1)} %select_bitcast_fusion), channel_id=1, source_target_pairs={{0,1},{1,0},{2,3},{3,2},{4,5},{5,4},{6,7},{7,6},{8,9},{9,8},{10,11... | collective-permute-start | bytes 3145736 | tf_op jit(solution)/shard_map/ppermute | solution.py:52
  122.9 5.5 %collective-permute-start.3 = (s32[128,2]{0,1:T(2,128)S(1)}, s32[128,2]{0,1:T(2,128)S(1)}, u32[]{:S(2)}, u32[]{:S(2)}) collective-permute-start(s32[128,2]{0,1:T(2,128)S(1)} %bitcast.190), channel_id=1, source_target_pairs={{8,0},{16,8},{24,16},{9,1},{17,9},{25,17},{10,2},{18,10},{26,18},{... | collective-permute-start | bytes 3080 | tf_op jit(solution)/shard_map/ppermute | solution.py:14
  128.8 13.3 %collective-permute-start.5 = (bf16[2,32,4096]{2,1,0:T(8,128)(2,1)S(1)}, bf16[2,32,4096]{2,1,0:T(8,128)(2,1)}, u32[]{:S(2)}, u32[]{:S(2)}) collective-permute-start(bf16[2,32,4096]{2,1,0:T(8,128)(2,1)S(1)} %select_bitcast_fusion.2), channel_id=1, source_target_pairs={{0,2},{1,3},{2,0},{3,1},{4,6},{5,7},{6,4},{7,5},{8,10},{9,11},{10,... | collective-permute-start | bytes 1572872 | tf_op jit(solution)/shard_map/ppermute | solution.py:52
  143.4 12.0 %collective-permute-start.7 = (bf16[32,4096]{1,0:T(8,128)(2,1)S(1)}, bf16[32,4096]{1,0:T(8,128)(2,1)S(1)}, u32[]{:S(2)}, u32[]{:S(2)}) collective-permute-start(bf16[32,4096]{1,0:T(8,128)(2,1)S(1)} %get-tuple-element.55), channel_id=1, source_target_pairs={{8,4},{9,5},{10,6},{11,7},{12,0},{13,1},{14,2},{15,3},{16,12},{17,... | collective-permute-start | bytes 786440 | tf_op jit(solution)/shard_map/ppermute | solution.py:75
  144.7 13.6 %collective-permute-start.6 = (bf16[32,4096]{1,0:T(8,128)(2,1)S(1)}, bf16[32,4096]{1,0:T(8,128)(2,1)S(1)}, u32[]{:S(2)}, u32[]{:S(2)}) collective-permute-start(bf16[32,4096]{1,0:T(8,128)(2,1)S(1)} %get-tuple-element.54), channel_id=1, source_target_pairs={{8,0},{9,1},{10,2},{11,3},{12,4},{13,5},{14,6},{15,7},{16,8},{17,9... | collective-permute-start | bytes 786440 | tf_op jit(solution)/shard_map/ppermute | solution.py:74
Sparse Core Ops, SparseCore 0:
  12.6 39.6 all-gather.1
where the time goes:
time: 168 us; the launch traced here: 167 us
  waiting for transfers between devices  78.3 us (47%)
  matrix products  52 us (31%)
  between operations  14.6 us (9%)
  starting transfers between devices  8.75 us (5%)
  local copies, waits for them, and re-layouts  6.88 us (4%)
  other arithmetic  6.58 us (4%)
    all_gather x1, waiting for transfers between devices, per_device(): lax.all_gather(packed, 'et', axis=0, tiled=True)  39.7 us
    ppermute x4, waiting for transfers between devices, halve_over_et(): got = lax.ppermute(give, 'et', [(i, i ^ bit) for i in range(n)])  18 us
    dot_general x2, matrix products, per_device(): lax.dot_general(d_up, up_mats[expert], (((1,), (1,)), ((), ())), preferre...  11.2 us
    dot_general x2, matrix products, per_device(): lax.dot_general(d_gate, gate_mats[expert], (((1,), (1,)), ((), ())), pref...  11.2 us
    dot_general x2, matrix products, per_device(): jnp.dot(hidden, down_mats[expert], preferred_element_type=jnp.float32)  9.21 us
    ppermute x1, waiting for transfers between devices, reduce_to_previous(): second = lax.ppermute(give, ('pipe', 'et'), to_other)  7.42 us
    dot_general x2, matrix products, per_device(): pre_up = jnp.dot(rows, up_mats[expert], preferred_element_type=jnp.float32)  6.48 us
    ppermute x1, waiting for transfers between devices, reduce_to_owner(): got = lax.ppermute(give, 'et', [(i, i ^ bit) for i in range(n)])  6.13 us
  transfers between devices with their start and end apart: 9, of which 7 were waited for; matrix products, arithmetic and copies ran while one was open for 18% of the time, Pallas kernels for 0%

commit v1 on v0

--- a/solution.py
+++ b/solution.py
@@ -1,3 +1,4 @@
+import functools
 import jax
 import jax.numpy as jnp
 from jax import lax
@@ -6,6 +7,30 @@
 E_WIN = 2
 MOST = 16
 TAIL = 128
+
+
+def pairs_all_push(local_block, axis_k):
+    plain, f_next, aux = (
+        jax.lax.psum(1, "et"),
+        jax.lax.axis_index("et"),
+        local_block.shape[axis_k],
+    )
+    buffer = tuple((ii * plain if t == axis_k else ii for t, ii in enumerate(local_block.shape)))
+    block_now = jnp.zeros(buffer, local_block.dtype)
+    k_now = lax.dynamic_update_slice_in_dim(block_now, local_block, f_next * aux, axis=axis_k)
+    idx = 1
+    while idx < plain:
+        local_block = jax.lax.ppermute(
+            local_block, "et", perm=tuple(((t, (t + 1) % plain) for t in range(plain)))
+        )
+        k_now = lax.dynamic_update_slice_in_dim(
+            k_now, local_block, (f_next - idx) % plain * aux, axis=axis_k
+        )
+        idx += 1
+    return k_now
+
+
+spread_the_pools = functools.partial(pairs_all_push, axis_k=0)
 
 
 def shifted(value, axis, steps):
@@ -101,9 +126,7 @@
     packed = jnp.concatenate(
         [pick_rows(select, local_rows), pick_rows(select, local_grads), weight_cols], axis=1
     )
-    gathered = lax.all_gather(packed, "et", axis=0, tiled=True).reshape(
-        n, E_WIN, MOST, 2 * width + TAIL
-    )
+    gathered = spread_the_pools(packed).reshape(n, E_WIN, MOST, 2 * width + TAIL)
     outs = []
     stored = []
     for expert in range(E_WIN):

time: 168 us -> 184 us (1.095)
  waiting for transfers between devices: 78.3 us -> 103 us
  between operations: 14.6 us -> 1.11 us
  local copies, waits for them, and re-layouts: 6.88 us -> 12.4 us
    ppermute x0 -> x7, waiting for transfers between devices: none -> 62.3 us  [pairs_all_push(): jax.lax.ppermute(local_block, 'et', perm=tuple(((t, (t + 1) % plain) for...]
    all_gather x1 -> x0, waiting for transfers between devices: 39.7 us -> none  [per_device(): lax.all_gather(packed, 'et', axis=0, tiled=True)]
    dynamic_update_slice x0 -> x7, local copies, waits for them, and re-layouts: none -> 5.86 us  [pairs_all_push(): lax.dynamic_update_slice_in_dim(k_now, local_block, (f_next - idx) % plai...]
    dot_general x2, matrix products: 6.48 us -> 2.53 us  [per_device(): pre_up = jnp.dot(rows, up_mats[expert], preferred_element_type=jnp.float32)]
    dot_general x2, matrix products: 3.33 us -> 6.96 us  [per_device(): jnp.dot(rows, gate_mats[expert], preferred_element_type=jnp.float32)]
    ppermute x4, starting transfers between devices: 3.46 us -> 1.12 us  [halve_over_et(): got = lax.ppermute(give, 'et', [(i, i ^ bit) for i in range(n)])]
    ppermute x4, waiting for transfers between devices: 18 us -> 20.3 us  [halve_over_et(): got = lax.ppermute(give, 'et', [(i, i ^ bit) for i in range(n)])]
    broadcast_in_dim x0 -> x1, local copies, waits for them, and re-layouts: none -> 2.25 us  [pairs_all_push(): block_now = jnp.zeros(buffer, local_block.dtype)]
  transfers between devices with their start and end apart: 9 -> 15, of which waited for: 7 -> 13; matrix products, arithmetic and copies ran while one was open for 18% -> 19% of each run, Pallas kernels for 0% -> 0%
where the time goes in v1:
time: 184 us
  waiting for transfers between devices  103 us (56%)
  matrix products  51.8 us (28%)
  local copies, waits for them, and re-layouts  12.4 us (7%)
  starting transfers between devices  7.81 us (4%)
  other arithmetic  7.5 us (4%)
    ppermute x7, waiting for transfers between devices, pairs_all_push(): jax.lax.ppermute(local_block, 'et', perm=tuple(((t, (t + 1) % plain) for...  62.3 us
    ppermute x4, waiting for transfers between devices, halve_over_et(): got = lax.ppermute(give, 'et', [(i, i ^ bit) for i in range(n)])  20.3 us
    dot_general x2, matrix products, per_device(): lax.dot_general(d_gate, gate_mats[expert], (((1,), (1,)), ((), ())), pref...  11.2 us
    dot_general x2, matrix products, per_device(): lax.dot_general(d_up, up_mats[expert], (((1,), (1,)), ((), ())), preferre...  11.1 us
    dot_general x2, matrix products, per_device(): jnp.dot(hidden, down_mats[expert], preferred_element_type=jnp.float32)  9.21 us
    ppermute x1, waiting for transfers between devices, reduce_to_previous(): second = lax.ppermute(give, ('pipe', 'et'), to_other)  7.42 us
    dot_general x2, matrix products, per_device(): jnp.dot(rows, gate_mats[expert], preferred_element_type=jnp.float32)  6.96 us
    dynamic_update_slice x7, local copies, waits for them, and re-layouts, pairs_all_push(): lax.dynamic_update_slice_in_dim(k_now, local_block, (f_next - idx) % plai...  5.86 us
  transfers between devices with their start and end apart: 15, of which 13 were waited for; matrix products, arithmetic and copies ran while one was open for 19% of the time, Pallas kernels for 0%

profile of v1, /device:TPU:0, one launch (start us, length us, event | category | flops | bytes accessed | tf_op | source)
XLA Modules:
  0.0 183.9 jit_solution(8991123186404990363)
XLA Ops:
  8.6 9.8 %collective-permute-done = bf16[32,8320]{1,0:T(8,128)(2,1)S(1)} collective-permute-done((bf16[32,8320]{1,0:T(8,128)(2,1)S(1)}, bf16[32,8320]{1,0:T(8,128)(2,1)S(1)}, u32[]{:S(2)}, u32[]{:S(2)}) %collective-permute-start) | collective-permute-done | bytes 532512 | tf_op jit(solution)/shard_map/ppermute | solution.py:23
  19.3 8.8 %collective-permute-done.1 = bf16[32,8320]{1,0:T(8,128)(2,1)S(1)} collective-permute-done((bf16[32,8320]{1,0:T(8,128)(2,1)S(1)}, bf16[32,8320]{1,0:T(8,128)(2,1)S(1)}, u32[]{:S(2)}, u32[]{:S(2)}) %collective-permute-start.1) | collective-permute-done | bytes 532512 | tf_op jit(solution)/shard_map/ppermute | solution.py:23
  28.9 8.8 %collective-permute-done.2 = bf16[32,8320]{1,0:T(8,128)(2,1)S(1)} collective-permute-done((bf16[32,8320]{1,0:T(8,128)(2,1)S(1)}, bf16[32,8320]{1,0:T(8,128)(2,1)S(1)}, u32[]{:S(2)}, u32[]{:S(2)}) %collective-permute-start.2) | collective-permute-done | bytes 532512 | tf_op jit(solution)/shard_map/ppermute | solution.py:23
  38.5 8.8 %collective-permute-done.3 = bf16[32,8320]{1,0:T(8,128)(2,1)S(1)} collective-permute-done((bf16[32,8320]{1,0:T(8,128)(2,1)S(1)}, bf16[32,8320]{1,0:T(8,128)(2,1)S(1)}, u32[]{:S(2)}, u32[]{:S(2)}) %collective-permute-start.3) | collective-permute-done | bytes 532512 | tf_op jit(solution)/shard_map/ppermute | solution.py:23
  48.0 8.8 %collective-permute-done.4 = bf16[32,8320]{1,0:T(8,128)(2,1)S(1)} collective-permute-done((bf16[32,8320]{1,0:T(8,128)(2,1)S(1)}, bf16[32,8320]{1,0:T(8,128)(2,1)S(1)}, u32[]{:S(2)}, u32[]{:S(2)}) %collective-permute-start.4) | collective-permute-done | bytes 532512 | tf_op jit(solution)/shard_map/ppermute | solution.py:23
  57.7 8.7 %collective-permute-done.5 = bf16[32,8320]{1,0:T(8,128)(2,1)S(1)} collective-permute-done((bf16[32,8320]{1,0:T(8,128)(2,1)S(1)}, bf16[32,8320]{1,0:T(8,128)(2,1)S(1)}, u32[]{:S(2)}, u32[]{:S(2)}) %collective-permute-start.5) | collective-permute-done | bytes 532512 | tf_op jit(solution)/shard_map/ppermute | solution.py:23
  67.3 8.7 %collective-permute-done.6 = bf16[32,8320]{1,0:T(8,128)(2,1)S(1)} collective-permute-done((bf16[32,8320]{1,0:T(8,128)(2,1)S(1)}, bf16[32,8320]{1,0:T(8,128)(2,1)S(1)}, u32[]{:S(2)}, u32[]{:S(2)}) %collective-permute-start.6) | collective-permute-done | bytes 532512 | tf_op jit(solution)/shard_map/ppermute | solution.py:23
  77.7 2.6 %fusion.103 = (bf16[8,1,16,4096]{3,2,1,0:T(8,128)(2,1)S(1)}, bf16[8,1,16,4096]{3,2,1,0:T(8,128)(2,1)S(1)}, bf16[8,1,16,4096]{3,2,1,0:T(8,128)(2,1)S(1)}, bf16[8,1,16,4096]{3,2,1,0:T(8,128)(2,1)S(1)}) fusion(bf16[8,2,16,8320]{3,2,1,0:T(8,128)(2,1)} %bitcast.7), kind=kLoop, calls=%fused_computation.142 | loop fusion | bytes 8388608 | tf_op jit(solution)/shard_map/slice | solution.py:147
  81.6 5.7 %fusion.10 = f32[128,896]{1,0:T(8,128)} fusion(bf16[128,4096]{1,0:T(8,128)(2,1)S(1)} %bitcast.179, bf16[1,2,4096,896]{3,2,1,0:T(8,128)(2,1)} %param.17), kind=kOutput, calls=%fused_computation.10 | convolution fusion | flops 939524096 | bytes 8847360 | tf_op jit(solution)/shard_map/dot_general | solution.py:135
  90.9 4.7 %fusion.48 = bf16[128,4096]{1,0:T(8,128)(2,1)S(1)} fusion(bf16[1,2,896,4096]{3,2,1,0:T(8,128)(2,1)} %param.19, f32[128]{0:T(128)S(1)} %reshape.401, f32[128,896]{1,0:T(8,128)S(1)} %fusion.6, f32[128,896]{1,0:T(8,128)} %fusion.10), kind=kOutput, calls=%fused_computation.40 | convolution fusion | flops 941260800 | bytes 9306624 | tf_op jit(solution)/shard_map/dot_general | solution.py:139
  95.6 4.5 %fusion.54 = bf16[128,4096]{1,0:T(8,128)(2,1)S(1)} fusion(bf16[1,2,896,4096]{3,2,1,0:T(8,128)(2,1)} %param.19, f32[128]{0:T(128)S(1)} %reshape.400, f32[128,896]{1,0:T(8,128)S(1)} %fusion.18, f32[128,896]{1,0:T(8,128)S(1)} %fusion.22), kind=kOutput, calls=%fused_computation.42 | convolution fusion | flops 941260800 | bytes 9306624 | tf_op jit(solution)/shard_map/dot_general | solution.py:139
  100.7 2.5 %fusion.65 = f32[128,896]{1,0:T(8,128)S(1)} fusion(bf16[128,4096]{1,0:T(8,128)(2,1)S(1)} %bitcast.175, bf16[1,2,896,4096]{3,2,1,0:T(8,128)(2,1)S(1)} %bitcast.182, f32[128]{0:T(128)S(1)} %reshape.401), kind=kOutput, calls=%fused_computation.55 | convolution fusion | flops 939638784 | bytes 8847872 | tf_op jit(solution)/shard_map/dot_general | solution.py:148
  103.2 5.5 %fusion.4 = f32[128,4096]{1,0:T(8,128)S(1)} fusion(bf16[1,2,4096,896]{3,2,1,0:T(8,128)(2,1)} %param.18, f32[128,896]{1,0:T(8,128)S(1)} %fusion.65, f32[128,896]{1,0:T(8,128)S(1)} %copy-done.4), kind=kOutput, calls=%fused_computation.4 | convolution fusion | flops 940212224 | bytes 10354688 | tf_op jit(solution)/shard_map/dot_general | solution.py:158
  108.8 2.7 %fusion.62 = f32[128,896]{1,0:T(8,128)S(1)} fusion(bf16[128,4096]{1,0:T(8,128)(2,1)S(1)} %bitcast.174, bf16[1,2,896,4096]{3,2,1,0:T(8,128)(2,1)S(1)} %bitcast.182, f32[128]{0:T(128)S(1)} %reshape.400), kind=kOutput, calls=%fused_computation.54 | convolution fusion | flops 939638784 | bytes 8847872 | tf_op jit(solution)/shard_map/dot_general | solution.py:148
  111.4 5.5 %fusion.16 = f32[128,4096]{1,0:T(8,128)S(1)} fusion(bf16[1,2,4096,896]{3,2,1,0:T(8,128)(2,1)} %param.18, f32[128,896]{1,0:T(8,128)S(1)} %fusion.62, f32[128,896]{1,0:T(8,128)S(1)} %fusion.22), kind=kOutput, calls=%fused_computation.16 | convolution fusion | flops 940212224 | bytes 10354688 | tf_op jit(solution)/shard_map/dot_general | solution.py:158
  117.0 5.6 %fusion.51 = bf16[128,4096]{1,0:T(8,128)(2,1)S(1)} fusion(f32[128,4096]{1,0:T(8,128)S(1)} %fusion.4, bf16[1,2,4096,896]{3,2,1,0:T(8,128)(2,1)} %param.17, f32[128,896]{1,0:T(8,128)S(1)} %copy-done.4, f32[128,896]{1,0:T(8,128)S(1)} %fusion.65, f32[128,896]{1,0:T(8,128)S(1)} %fusion.6), kind=kOutput, calls=%fused_computation.41 | convolution fusion | flops 941719552 | bytes 11862016 | tf_op jit(solution)/shard_map/dot_general | solution.py:156
  123.3 5.6 %fusion.57 = bf16[128,4096]{1,0:T(8,128)(2,1)S(1)} fusion(f32[128,4096]{1,0:T(8,128)S(1)} %fusion.16, bf16[1,2,4096,896]{3,2,1,0:T(8,128)(2,1)} %param.17, f32[128,896]{1,0:T(8,128)S(1)} %fusion.22, f32[128,896]{1,0:T(8,128)S(1)} %fusion.62, f32[128,896]{1,0:T(8,128)S(1)} %fusion.18), kind=kOutput, calls=%fused_computation.43 | convolution fusion | flops 941719552 | bytes 11862016 | tf_op jit(solution)/shard_map/dot_general | solution.py:156
  128.9 8.3 %collective-permute-done.8 = bf16[2,32,4096]{2,1,0:T(8,128)(2,1)S(1)} collective-permute-done((bf16[2,32,4096]{2,1,0:T(8,128)(2,1)S(1)}, bf16[2,32,4096]{2,1,0:T(8,128)(2,1)S(1)}, u32[]{:S(2)}, u32[]{:S(2)}) %collective-permute-start.8) | collective-permute-done | bytes 524320 | tf_op jit(solution)/shard_map/ppermute | solution.py:77
  137.5 2.3 %collective-permute-start.9 = (bf16[32,4096]{1,0:T(8,128)(2,1)S(1)}, bf16[32,4096]{1,0:T(8,128)(2,1)S(1)}, u32[]{:S(2)}, u32[]{:S(2)}) collective-permute-start(bf16[32,4096]{1,0:T(8,128)(2,1)S(1)} %select_bitcast_fusion.6), channel_id=1, source_target_pairs={{0,4},{1,5},{2,6},{3,7},{4,0},{5,1},{6,2},{7,3},{8,12},{9,13},{10,... | collective-permute-start | bytes 786440 | tf_op jit(solution)/shard_map/ppermute | solution.py:87
  140.0 5.8 %collective-permute-done.9 = bf16[32,4096]{1,0:T(8,128)(2,1)S(1)} collective-permute-done((bf16[32,4096]{1,0:T(8,128)(2,1)S(1)}, bf16[32,4096]{1,0:T(8,128)(2,1)S(1)}, u32[]{:S(2)}, u32[]{:S(2)}) %collective-permute-start.9) | collective-permute-done | bytes 262176 | tf_op jit(solution)/shard_map/ppermute | solution.py:87
  147.4 4.2 %collective-permute-done.10 = s32[128,2]{0,1:T(2,128)S(1)} collective-permute-done((s32[128,2]{0,1:T(2,128)S(1)}, s32[128,2]{0,1:T(2,128)S(1)}, u32[]{:S(2)}, u32[]{:S(2)}) %collective-permute-start.10) | collective-permute-done | bytes 1056 | tf_op jit(solution)/shard_map/ppermute | solution.py:39
  153.4 12.0 %collective-permute-done.12 = bf16[2,32,4096]{2,1,0:T(8,128)(2,1)} collective-permute-done((bf16[2,32,4096]{2,1,0:T(8,128)(2,1)S(1)}, bf16[2,32,4096]{2,1,0:T(8,128)(2,1)}, u32[]{:S(2)}, u32[]{:S(2)}) %collective-permute-start.12) | collective-permute-done | bytes 524320 | tf_op jit(solution)/shard_map/ppermute | solution.py:77
  171.3 7.4 %collective-permute-done.14 = bf16[32,4096]{1,0:T(8,128)(2,1)S(1)} collective-permute-done((bf16[32,4096]{1,0:T(8,128)(2,1)S(1)}, bf16[32,4096]{1,0:T(8,128)(2,1)S(1)}, u32[]{:S(2)}, u32[]{:S(2)}) %collective-permute-start.14) | collective-permute-done | bytes 262176 | tf_op jit(solution)/shard_map/ppermute | solution.py:100
  178.7 3.2 %collective-permute-done.13 = bf16[32,4096]{1,0:T(8,128)(2,1)S(1)} collective-permute-done((bf16[32,4096]{1,0:T(8,128)(2,1)S(1)}, bf16[32,4096]{1,0:T(8,128)(2,1)S(1)}, u32[]{:S(2)}, u32[]{:S(2)}) %collective-permute-start.13) | collective-permute-done | bytes 262176 | tf_op jit(solution)/shard_map/ppermute | solution.py:99
  (100 shorter events, 32.4 us)
Async XLA Ops:
  8.1 10.3 %collective-permute-start = (bf16[32,8320]{1,0:T(8,128)(2,1)S(1)}, bf16[32,8320]{1,0:T(8,128)(2,1)S(1)}, u32[]{:S(2)}, u32[]{:S(2)}) collective-permute-start(bf16[32,8320]{1,0:T(8,128)(2,1)S(1)} %get-tuple-element.54), channel_id=1, source_target_pairs={{0,1},{1,2},{2,3},{3,4},{4,5},{5,6},{6,7},{7,0},{8,9},{9,10},{10,1... | collective-permute-start | bytes 1597448 | tf_op jit(solution)/shard_map/ppermute | solution.py:23
  18.4 9.6 %collective-permute-start.1 = (bf16[32,8320]{1,0:T(8,128)(2,1)S(1)}, bf16[32,8320]{1,0:T(8,128)(2,1)S(1)}, u32[]{:S(2)}, u32[]{:S(2)}) collective-permute-start(bf16[32,8320]{1,0:T(8,128)(2,1)S(1)} %collective-permute-done), channel_id=1, source_target_pairs={{0,1},{1,2},{2,3},{3,4},{4,5},{5,6},{6,7},{7,0},{8,9},{9,10},{10,1... | collective-permute-start | bytes 1597448 | tf_op jit(solution)/shard_map/ppermute | solution.py:23
  28.0 9.6 %collective-permute-start.2 = (bf16[32,8320]{1,0:T(8,128)(2,1)S(1)}, bf16[32,8320]{1,0:T(8,128)(2,1)S(1)}, u32[]{:S(2)}, u32[]{:S(2)}) collective-permute-start(bf16[32,8320]{1,0:T(8,128)(2,1)S(1)} %collective-permute-done.1), channel_id=1, source_target_pairs={{0,1},{1,2},{2,3},{3,4},{4,5},{5,6},{6,7},{7,0},{8,9},{9,10},{10,1... | collective-permute-start | bytes 1597448 | tf_op jit(solution)/shard_map/ppermute | solution.py:23
  28.0 52.3 %copy-start.3 = (bf16[1,2,4096,896]{3,2,1,0:T(8,128)(2,1)S(1)}, bf16[1,2,4096,896]{3,2,1,0:T(8,128)(2,1)}, u32[]{:S(2)}) copy-start(bf16[1,2,4096,896]{3,2,1,0:T(8,128)(2,1)} %param.18) | copy-start | bytes 44040196
  37.6 9.6 %collective-permute-start.3 = (bf16[32,8320]{1,0:T(8,128)(2,1)S(1)}, bf16[32,8320]{1,0:T(8,128)(2,1)S(1)}, u32[]{:S(2)}, u32[]{:S(2)}) collective-permute-start(bf16[32,8320]{1,0:T(8,128)(2,1)S(1)} %collective-permute-done.2), channel_id=1, source_target_pairs={{0,1},{1,2},{2,3},{3,4},{4,5},{5,6},{6,7},{7,0},{8,9},{9,10},{10,1... | collective-permute-start | bytes 1597448 | tf_op jit(solution)/shard_map/ppermute | solution.py:23
  47.2 9.6 %collective-permute-start.4 = (bf16[32,8320]{1,0:T(8,128)(2,1)S(1)}, bf16[32,8320]{1,0:T(8,128)(2,1)S(1)}, u32[]{:S(2)}, u32[]{:S(2)}) collective-permute-start(bf16[32,8320]{1,0:T(8,128)(2,1)S(1)} %collective-permute-done.3), channel_id=1, source_target_pairs={{0,1},{1,2},{2,3},{3,4},{4,5},{5,6},{6,7},{7,0},{8,9},{9,10},{10,1... | collective-permute-start | bytes 1597448 | tf_op jit(solution)/shard_map/ppermute | solution.py:23
  56.8 9.6 %collective-permute-start.5 = (bf16[32,8320]{1,0:T(8,128)(2,1)S(1)}, bf16[32,8320]{1,0:T(8,128)(2,1)S(1)}, u32[]{:S(2)}, u32[]{:S(2)}) collective-permute-start(bf16[32,8320]{1,0:T(8,128)(2,1)S(1)} %collective-permute-done.4), channel_id=1, source_target_pairs={{0,1},{1,2},{2,3},{3,4},{4,5},{5,6},{6,7},{7,0},{8,9},{9,10},{10,1... | collective-permute-start | bytes 1597448 | tf_op jit(solution)/shard_map/ppermute | solution.py:23
  66.4 9.6 %collective-permute-start.6 = (bf16[32,8320]{1,0:T(8,128)(2,1)S(1)}, bf16[32,8320]{1,0:T(8,128)(2,1)S(1)}, u32[]{:S(2)}, u32[]{:S(2)}) collective-permute-start(bf16[32,8320]{1,0:T(8,128)(2,1)S(1)} %collective-permute-done.5), channel_id=1, source_target_pairs={{0,1},{1,2},{2,3},{3,4},{4,5},{5,6},{6,7},{7,0},{8,9},{9,10},{10,1... | collective-permute-start | bytes 1597448 | tf_op jit(solution)/shard_map/ppermute | solution.py:23
  80.3 8.3 %slice-start.4 = ((s8[14680064]{0:T(1024)(128)(4,1)}), s8[4194304]{0:T(1024)(128)(4,1)S(1)}, s32[]{:S(2)}) async-start(s8[14680064]{0:T(1024)(128)(4,1)} %bitcast.183), calls=%async_computation.4 | async-start | bytes 8388608
  80.3 8.3 %slice-start.5 = ((s8[14680064]{0:T(1024)(128)(4,1)}), s8[2097152]{0:T(1024)(128)(4,1)S(1)}, s32[]{:S(2)}) async-start(s8[14680064]{0:T(1024)(128)(4,1)} %bitcast.183), calls=%async_computation.5 | async-start | bytes 4194304
  81.6 7.0 %slice-start.6 = ((s8[14680064]{0:T(1024)(128)(4,1)}), s8[4194304]{0:T(1024)(128)(4,1)S(1)}, s32[]{:S(2)}) async-start(s8[14680064]{0:T(1024)(128)(4,1)} %bitcast.183), calls=%async_computation.6 | async-start | bytes 8388608
  90.9 9.7 %slice-start = ((s8[14680064]{0:T(1024)(128)(4,1)}), s8[4194304]{0:T(1024)(128)(4,1)S(1)}, s32[]{:S(2)}) async-start(s8[14680064]{0:T(1024)(128)(4,1)} %bitcast.181), calls=%async_computation | async-start | bytes 8388608
  90.9 9.7 %slice-start.1 = ((s8[14680064]{0:T(1024)(128)(4,1)}), s8[4194304]{0:T(1024)(128)(4,1)S(1)}, s32[]{:S(2)}) async-start(s8[14680064]{0:T(1024)(128)(4,1)} %bitcast.181), calls=%async_computation.1 | async-start | bytes 8388608
  95.6 5.1 %slice-start.3 = ((s8[14680064]{0:T(1024)(128)(4,1)}), s8[2097152]{0:T(1024)(128)(4,1)S(1)}, s32[]{:S(2)}) async-start(s8[14680064]{0:T(1024)(128)(4,1)} %bitcast.181), calls=%async_computation.3 | async-start | bytes 4194304
  100.5 22.1 %collective-permute-start.7 = (bf16[4,32,4096]{2,1,0:T(8,128)(2,1)S(1)}, bf16[4,32,4096]{2,1,0:T(8,128)(2,1)S(1)}, u32[]{:S(2)}, u32[]{:S(2)}) collective-permute-start(bf16[4,32,4096]{2,1,0:T(8,128)(2,1)S(1)} %select_bitcast_fusion.1), channel_id=1, source_target_pairs={{0,1},{1,0},{2,3},{3,2},{4,5},{5,4},{6,7},{7,6},{8,9},{9,8},{10,11... | collective-permute-start | bytes 3145736 | tf_op jit(solution)/shard_map/ppermute | solution.py:77
  123.0 14.3 %collective-permute-start.8 = (bf16[2,32,4096]{2,1,0:T(8,128)(2,1)S(1)}, bf16[2,32,4096]{2,1,0:T(8,128)(2,1)S(1)}, u32[]{:S(2)}, u32[]{:S(2)}) collective-permute-start(bf16[2,32,4096]{2,1,0:T(8,128)(2,1)S(1)} %select_bitcast_fusion.3), channel_id=1, source_target_pairs={{0,2},{1,3},{2,0},{3,1},{4,6},{5,7},{6,4},{7,5},{8,10},{9,11},{10,... | collective-permute-start | bytes 1572872 | tf_op jit(solution)/shard_map/ppermute | solution.py:77
  137.4 8.7 %copy-start.2 = (s32[1,128,2]{1,2,0:T(2,128)S(1)}, s32[1,128,2]{1,2,0:T(2,128)}, u32[]{:S(2)}) copy-start(s32[1,128,2]{1,2,0:T(2,128)} %param.15) | copy-start | bytes 3076
  137.5 8.4 %collective-permute-start.9 = (bf16[32,4096]{1,0:T(8,128)(2,1)S(1)}, bf16[32,4096]{1,0:T(8,128)(2,1)S(1)}, u32[]{:S(2)}, u32[]{:S(2)}) collective-permute-start(bf16[32,4096]{1,0:T(8,128)(2,1)S(1)} %select_bitcast_fusion.6), channel_id=1, source_target_pairs={{0,4},{1,5},{2,6},{3,7},{4,0},{5,1},{6,2},{7,3},{8,12},{9,13},{10,... | collective-permute-start | bytes 786440 | tf_op jit(solution)/shard_map/ppermute | solution.py:87
  146.0 5.6 %collective-permute-start.11 = (bf16[4,32,4096]{2,1,0:T(8,128)(2,1)S(1)}, bf16[4,32,4096]{2,1,0:T(8,128)(2,1)S(1)}, u32[]{:S(2)}, u32[]{:S(2)}) collective-permute-start(bf16[4,32,4096]{2,1,0:T(8,128)(2,1)S(1)} %select_bitcast_fusion), channel_id=1, source_target_pairs={{0,1},{1,0},{2,3},{3,2},{4,5},{5,4},{6,7},{7,6},{8,9},{9,8},{10,11... | collective-permute-start | bytes 3145736 | tf_op jit(solution)/shard_map/ppermute | solution.py:77
  146.1 5.5 %collective-permute-start.10 = (s32[128,2]{0,1:T(2,128)S(1)}, s32[128,2]{0,1:T(2,128)S(1)}, u32[]{:S(2)}, u32[]{:S(2)}) collective-permute-start(s32[128,2]{0,1:T(2,128)S(1)} %bitcast.180), channel_id=1, source_target_pairs={{8,0},{16,8},{24,16},{9,1},{17,9},{25,17},{10,2},{18,10},{26,18},{... | collective-permute-start | bytes 3080 | tf_op jit(solution)/shard_map/ppermute | solution.py:39
  151.6 32.3 %copy-start.1 = (bf16[1,128,4096]{2,1,0:T(8,128)(2,1)S(1)}, bf16[1,128,4096]{2,1,0:T(8,128)(2,1)}, u32[]{:S(2)}) copy-start(bf16[1,128,4096]{2,1,0:T(8,128)(2,1)} %param.16) | copy-start | bytes 3145732
  152.0 13.4 %collective-permute-start.12 = (bf16[2,32,4096]{2,1,0:T(8,128)(2,1)S(1)}, bf16[2,32,4096]{2,1,0:T(8,128)(2,1)}, u32[]{:S(2)}, u32[]{:S(2)}) collective-permute-start(bf16[2,32,4096]{2,1,0:T(8,128)(2,1)S(1)} %select_bitcast_fusion.2), channel_id=1, source_target_pairs={{0,2},{1,3},{2,0},{3,1},{4,6},{5,7},{6,4},{7,5},{8,10},{9,11},{10,... | collective-permute-start | bytes 1572872 | tf_op jit(solution)/shard_map/ppermute | solution.py:77
  166.7 12.0 %collective-permute-start.14 = (bf16[32,4096]{1,0:T(8,128)(2,1)S(1)}, bf16[32,4096]{1,0:T(8,128)(2,1)S(1)}, u32[]{:S(2)}, u32[]{:S(2)}) collective-permute-start(bf16[32,4096]{1,0:T(8,128)(2,1)S(1)} %get-tuple-element.57), channel_id=1, source_target_pairs={{8,4},{9,5},{10,6},{11,7},{12,0},{13,1},{14,2},{15,3},{16,12},{17,... | collective-permute-start | bytes 786440 | tf_op jit(solution)/shard_map/ppermute | solution.py:100
  168.0 13.9 %collective-permute-start.13 = (bf16[32,4096]{1,0:T(8,128)(2,1)S(1)}, bf16[32,4096]{1,0:T(8,128)(2,1)S(1)}, u32[]{:S(2)}, u32[]{:S(2)}) collective-permute-start(bf16[32,4096]{1,0:T(8,128)(2,1)S(1)} %get-tuple-element.56), channel_id=1, source_target_pairs={{8,0},{9,1},{10,2},{11,3},{12,4},{13,5},{14,6},{15,7},{16,8},{17,9... | collective-permute-start | bytes 786440 | tf_op jit(solution)/shard_map/ppermute | solution.py:99
  (4 other events, 12.0 us)
